TPU v7x, 32 devices: a whole 2x2x4 slice. The times are simulated.
32 devices in a mesh: tm: 4 (over y, x), height: 2 (over core), chan: 4 (over z).
Axes of the slice: x: 2, y: 2, z: 4, core: 2. Of those that a mesh axis runs over, the one named last changes fastest.
Arguments:
- features: bfloat16 [384, 8, 8, 160], P('chan', 'tm', 'height'), may hold values from -400 to 400, as said below
- cotangent: bfloat16 [384, 8, 8, 160], P('chan', 'tm', 'height'), may hold values from -6 to 6
- conv_weight: bfloat16 [384, 27, 384], P('chan'), may hold values from -0.0625 to 0.0625
- norm_gain: float32 [384], replicated, may hold values from 0.5 to 1.5
- norm_bias: float32 [384], replicated, may hold values from -3 to 3
Outputs:
- input_grad: bfloat16 [384, 8, 8, 160], P('chan', 'tm', 'height')
- weight_grad: float32 [384, 27, 384], P('chan')
Inputs may be any that keep to these rules, and one draw needn't show every extreme that they name: `features`: bounded activations.
All inputs are finite; a program needn't handle non-finite values.
Results may differ from a plain program's by a relative error of at most 0.003.
Values may be sent and summed in bfloat16 or wider, within the bound.
No kernel may reach another device: no remote copies, remote signals or barrier semaphores. Data moves between devices by JAX's collectives and lax.ppermute only.
A program may use at most 64 MiB of HBM per device.

v0:
```python
import math
import jax
import jax.numpy as jnp
from jax import lax
from jax.sharding import PartitionSpec as P


def from_behind(block, axis, distance):
    devices = range(lax.axis_size(axis))
    route = [(i - distance, i) for i in devices if i - distance in devices]
    return lax.ppermute(block, axis, route)


def with_halo(array, sides, width):
    for axis, dim in sides:
        size, length = (lax.axis_size(axis), array.shape[dim])
        up = [(i, (i + 1) % size) for i in range(size - 1)]
        down = [(j, i) for i, j in up]
        last = lax.slice_in_dim(array, length - width, length, axis=dim)
        first = lax.slice_in_dim(array, 0, width, axis=dim)
        before = lax.ppermute(last, axis, up)
        after = lax.ppermute(first, axis, down)
        array = jnp.concatenate([before, array, after], axis=dim)
    return array


def on_device(features, cotangent, conv_weight, norm_gain, norm_bias):
    chans, frames, rows, cols = features.shape
    whole_x = lax.all_gather(features, "chan", axis=0, tiled=True)
    total = whole_x.shape[0]
    flat_x = whole_x.reshape(total, -1).astype(jnp.float32)
    inv_rms = lax.rsqrt(jnp.mean(flat_x * flat_x, axis=0, keepdims=True) + 1e-06)
    normed = flat_x * inv_rms * norm_gain[:, None] + norm_bias[:, None]
    active = jax.nn.silu(normed).astype(jnp.bfloat16)
    ahead = from_behind(cotangent, "tm", -1)
    longer = jnp.concatenate([cotangent, ahead], axis=1)
    bordered = with_halo(longer, (("height", 2),), 1)
    padded = jnp.pad(bordered, ((0, 0), (0, 0), (0, 0), (1, 1)))
    taps = []
    for kt in range(3):
        for kh in range(3):
            for kw in range(3):
                taps.append(
                    padded[
                        :, 2 - kt : 2 - kt + frames, 2 - kh : 2 - kh + rows, 2 - kw : 2 - kw + cols
                    ]
                )
    stacked = jnp.stack(taps, axis=1).reshape(chans * 27, -1)
    local_sums = lax.dot_general(
        stacked, active, (((1,), (1,)), ((), ())), preferred_element_type=jnp.float32
    )
    positions = frames * lax.axis_size("tm") * rows * lax.axis_size("height") * cols
    summed = lax.psum(local_sums, ("tm", "height"))
    weight_grad = (summed / math.sqrt(positions)).reshape(chans, 27, total)
    sig = jax.nn.sigmoid(normed)
    slope = sig * (1.0 + normed * (1.0 - sig))
    offset = lax.axis_index("chan") * chans
    weight_part = conv_weight.reshape(chans * 27, chans * lax.axis_size("chan"))
    act_grad = lax.psum_scatter(
        lax.dot_general(
            weight_part, stacked, (((0,), (0,)), ((), ())), preferred_element_type=jnp.float32
        ),
        "chan",
        scatter_dimension=0,
        tiled=True,
    )
    own_x = features.reshape(chans, -1).astype(jnp.float32)
    own_slope = lax.dynamic_slice_in_dim(slope, offset, chans, 0)
    own_gain = lax.dynamic_slice_in_dim(norm_gain, offset, chans, 0)
    upstream = act_grad * own_slope * own_gain[:, None]
    dots = lax.psum(jnp.sum(upstream * own_x, axis=0, keepdims=True), "chan")
    own_back = inv_rms * upstream - own_x * inv_rms**3 * dots / total
    result = cotangent.reshape(chans, -1).astype(jnp.float32) + own_back
    return (result.astype(jnp.bfloat16).reshape(features.shape), weight_grad)


def solution(mesh):
    return jax.shard_map(
        on_device,
        mesh=mesh,
        in_specs=(
            P("chan", "tm", "height", None),
            P("chan", "tm", "height", None),
            P("chan", None, None),
            P(),
            P(),
        ),
        out_specs=(P("chan", "tm", "height", None), P("chan", None, None)),
        check_vma=False,
    )
```

profile of v0, /device:TPU:0, one launch (start us, length us, event | category | flops | bytes accessed | tf_op | source)
XLA Modules:
  0.0 245.2 jit_solution(13448478375143645336)
XLA Ops:
  8.0 1.3 collective-permute-start
  9.3 1.3 copy.16
  10.7 31.4 %all_gather.3 = bf16[384,2,4,160]{3,2,1,0:T(4,128)(2,1)S(1)} all-gather(bf16[96,2,4,160]{3,2,1,0:T(4,128)(2,1)S(1)} %copy.16), channel_id=1, replica_groups=mesh['tm'=4,'height'=2,'chan'=4] {'chan'}, dimensions={0}, use_global_device_ids=true | all-gather | bytes 1228800 | tf_op jit(solution)/shard_map/all_gather | solution.py:29
  42.1 1.4 copy.17
  43.9 1.0 constant_dynamic-update-slice_fusion.1
  45.0 1.3 collective-permute-start.1
  46.3 1.3 collective-permute-start.2
  47.6 1.4 multiply_convert_fusion
  50.0 0.8 fusion.53
  50.8 0.8 fusion.30
  52.4 0.8 fusion.51
  53.9 0.8 fusion.50
  54.7 0.8 fusion.49
  55.5 0.8 fusion.24
  56.3 0.8 fusion.48
  57.1 0.8 fusion.47
  57.9 0.8 fusion.27
  59.5 0.8 fusion.45
  60.3 0.8 fusion.44
  61.1 0.8 fusion.43
  61.8 0.8 fusion.42
  62.6 0.8 fusion.21
  63.4 0.8 fusion.41
  64.2 0.8 fusion.40
  65.0 0.8 fusion.39
  65.8 0.8 fusion.37
  66.6 0.8 fusion.36
  67.4 0.7 bitcast_dynamic-update-slice_fusion
  68.2 0.8 fusion.35
  68.9 0.8 fusion.34
  69.7 0.8 fusion.33
  70.6 0.8 fusion.31
  71.3 21.1 %copy.18 = bf16[96,27,2,4,160]{4,3,2,1,0:T(4,128)(2,1)} copy(bf16[96,27,2,4,160]{0,4,3,2,1:T(8,128)(2,1)} %fusion.31) | data formatting | bytes 13271040 | tf_op jit(solution)/shard_map/stack | solution.py:48
  92.5 20.4 %reshape.67 = bf16[2592,1280]{1,0:T(8,128)(2,1)} reshape(bf16[96,27,2,4,160]{4,3,2,1,0:T(4,128)(2,1)} %copy.18) | data formatting | bytes 13271040 | tf_op jit(solution)/shard_map/reshape | solution.py:48
  112.8 8.4 %fusion.56 = f32[2592,384]{1,0:T(8,128)} fusion(bf16[2592,1280]{1,0:T(8,128)(2,1)} %reshape.67, bf16[384,1280]{0,1:T(8,128)(2,1)S(1)} %bitcast.128), kind=kOutput, calls=%fused_computation.102 | convolution fusion | flops 2548039680 | bytes 11599872 | tf_op jit(solution)/shard_map/dot_general | solution.py:49
  121.5 2.3 copy.19
  123.8 2.2 reshape.68
  126.0 6.7 %convolution_bitcast_fusion = f32[384,1280]{0,1:T(8,128)S(1)} fusion(bf16[2592,1280]{1,0:T(8,128)(2,1)} %reshape.67, bf16[2592,384]{1,0:T(8,128)(2,1)} %reshape.68), kind=kOutput, calls=%fused_computation.2 | convolution fusion | flops 2548039680 | bytes 10592256 | tf_op jit(solution)/shard_map/dot_general | solution.py:60
  132.7 1.8 copy.21
  134.7 1.8 negate_exponential_fusion
  136.5 66.4 %all-reduce.3.cloned.1.call-done = f32[2592,384]{1,0:T(8,128)} async-done(((f32[2592,384]{1,0:T(8,128)}), f32[2592,384]{1,0:T(8,128)}) %all-reduce.3.cloned.1.call-update) | async-done | bytes 3981328 | tf_op jit(solution)/shard_map/psum | solution.py:53
  202.9 4.4 %broadcast_multiply_fusion = f32[2592,384]{1,0:T(8,128)} fusion(f32[2592,384]{1,0:T(8,128)} %all-reduce.3.cloned.1.call-done), kind=kLoop, calls=%fused_computation.4 | loop fusion | flops 995328 | bytes 7962624 | tf_op jit(solution)/shard_map/div | solution.py:54
  207.3 5.0 %reshape.70 = f32[96,27,384]{2,1,0:T(8,128)} reshape(f32[2592,384]{1,0:T(8,128)} %broadcast_multiply_fusion) | data formatting | bytes 7962624 | tf_op jit(solution)/shard_map/reshape | solution.py:54
  212.3 6.6 %copy.20 = f32[96,27,384]{2,0,1:T(8,128)} copy(f32[96,27,384]{2,1,0:T(8,128)} %reshape.70) | data formatting | bytes 7962624
  218.8 2.1 copy.22
  221.0 2.8 %fusion.13 = (f32[1280]{0:T(1024)S(1)}, f32[96,1280]{0,1:T(8,128)}) fusion(bf16[96,2,4,160]{0,3,2,1:T(8,128)(2,1)S(1)} %copy-done.2, f32[96]{0:T(128)S(1)} %dynamic_slice.7, f32[96,1280]{0,1:T(8,128)} %copy.22, f32[384,1280]{0,1:T(8,128)} %get-tuple-element.13, s32[]{:T(128)S(6)} %select_n.4, f32[384,1280]{0,1:T(8,128)S(1)} %get-tuple-element.12), kind=kLoop, calls=%fused_computation.31 | loop fusion | flops 1350400 | bytes 2217348 | tf_op jit(solution)/shard_map/reduce_sum | solution.py:71
  223.8 11.6 %psum.14 = f32[1280]{0:T(1024)S(1)} all-reduce(f32[1280]{0:T(1024)S(1)} %get-tuple-element.10), channel_id=1, replica_groups=mesh['tm'=4,'height'=2,'chan'=4] {'chan'}, use_global_device_ids=true, to_apply=%region_3.4 | all-reduce | flops 1280 | bytes 10240 | tf_op jit(solution)/shard_map/psum | solution.py:71
  235.4 2.4 fusion.12
  (29 shorter events, 4.1 us)
Async XLA Ops:
  8.0 194.9 %all-reduce.3.cloned.1.call-start = ((), (), s32[]{:S(2)}) async-start(), calls=%async_computation.1 | async-start | bytes 7962624 | tf_op jit(solution)/shard_map/psum | solution.py:53
  8.0 36.9 %collective-permute-start = (bf16[96,2,4,160]{0,3,2,1:T(8,128)(2,1)}, bf16[96,2,4,160]{0,3,2,1:T(8,128)(2,1)S(1)}, u32[]{:S(2)}, u32[]{:S(2)}) collective-permute-start(bf16[96,2,4,160]{0,3,2,1:T(8,128)(2,1)} %param.6), channel_id=1, source_target_pairs={{8,0},{16,8},{24,16},{9,1},{17,9},{25,17},{10,2},{18,10},{26,18},{... | collective-permute-start | bytes 737288 | tf_op jit(solution)/shard_map/ppermute | solution.py:11
  45.0 4.0 %collective-permute-start.1 = (bf16[96,4,1,160]{0,3,2,1:T(8,128)(2,1)S(1)}, bf16[96,4,1,160]{0,3,2,1:T(8,128)(2,1)S(1)}, u32[]{:S(2)}, u32[]{:S(2)}) collective-permute-start(bf16[96,4,1,160]{0,3,2,1:T(8,128)(2,1)S(1)} %get-tuple-element.14), channel_id=1, source_target_pairs={{0,4},{1,5},{2,6},{3,7},{8,12},{9,13},{10,14},{11,15},{16,20},{17,... | collective-permute-start | bytes 368648 | tf_op jit(solution)/shard_map/ppermute | solution.py:21
  46.3 3.3 %collective-permute-start.2 = (bf16[96,4,1,160]{0,3,2,1:T(8,128)(2,1)S(1)}, bf16[96,4,1,160]{0,3,2,1:T(8,128)(2,1)S(1)}, u32[]{:S(2)}, u32[]{:S(2)}) collective-permute-start(bf16[96,4,1,160]{0,3,2,1:T(8,128)(2,1)S(1)} %get-tuple-element.15), channel_id=1, source_target_pairs={{4,0},{5,1},{6,2},{7,3},{12,8},{13,9},{14,10},{15,11},{20,16},{21,... | collective-permute-start | bytes 368648 | tf_op jit(solution)/shard_map/ppermute | solution.py:22
  50.0 17.4 %copy-start = (bf16[96,2,4,160]{0,3,2,1:T(8,128)(2,1)S(1)}, bf16[96,2,4,160]{0,3,2,1:T(8,128)(2,1)}, u32[]{:S(2)}) copy-start(bf16[96,2,4,160]{0,3,2,1:T(8,128)(2,1)} %param.6) | copy-start | bytes 737284
  121.3 97.5 %reduce-scatter.4.cloned.1.call-start = ((), (), s32[]{:S(2)}) async-start(), calls=%async_computation.2 | async-start | bytes 2457600
  126.0 8.6 %copy-start.3 = (f32[384]{0:T(512)S(1)}, f32[384]{0:T(512)}, u32[]{:S(2)}) copy-start(f32[384]{0:T(512)} %param.8) | copy-start | bytes 4612
  126.0 8.7 %copy-start.4 = (f32[384]{0:T(512)S(1)}, f32[384]{0:T(512)}, u32[]{:S(2)}) copy-start(f32[384]{0:T(512)} %param.9) | copy-start | bytes 4612
  207.3 13.7 %copy-start.2 = (bf16[96,2,4,160]{0,3,2,1:T(8,128)(2,1)S(1)}, bf16[96,2,4,160]{0,3,2,1:T(8,128)(2,1)}, u32[]{:S(2)}) copy-start(bf16[96,2,4,160]{0,3,2,1:T(8,128)(2,1)} %param.5) | copy-start | bytes 737284
  207.3 28.1 %copy-start.1 = (bf16[96,2,4,160]{0,3,2,1:T(8,128)(2,1)S(1)}, bf16[96,2,4,160]{0,3,2,1:T(8,128)(2,1)}, u32[]{:S(2)}) copy-start(bf16[96,2,4,160]{0,3,2,1:T(8,128)(2,1)} %param.6) | copy-start | bytes 737284
Sparse Core Ops, SparseCore 0:
  121.4 81.3 all-reduce.2
Sparse Core Ops, SparseCore 1:
  134.6 44.6 reduce-scatter.3
where the time goes:
time: 247 us; the launch traced here: 245 us
  local copies, waits for them, and re-layouts  82 us (33%)
  waiting for transfers between devices  67 us (27%)
  blocking collectives  43 us (17%)
  other arithmetic  18.3 us (7%)
  between operations  15.6 us (6%)
  matrix products  15.1 us (6%)
  starting transfers between devices  4.15 us (2%)
    psum x1, waiting for transfers between devices, on_device(): summed = lax.psum(local_sums, ('tm', 'height'))  66.4 us
    all_gather x1, blocking collectives, on_device(): whole_x = lax.all_gather(features, 'chan', axis=0, tiled=True)  31.4 us
    unnamed x36, local copies, waits for them, and re-layouts  30.9 us
    another operation x2, local copies, waits for them, and re-layouts, on_device(): stacked = jnp.stack(taps, axis=1).reshape(chans * 27, -1)  21.9 us
    reshape x1, local copies, waits for them, and re-layouts, on_device(): stacked = jnp.stack(taps, axis=1).reshape(chans * 27, -1)  20.4 us
    psum x1, blocking collectives, on_device(): dots = lax.psum(jnp.sum(upstream * own_x, axis=0, keepdims=True), 'chan')  11.6 us
    dot_general x1, matrix products, on_device(): lax.dot_general(stacked, active, (((1,), (1,)), ((), ())), preferred_elem...  8.42 us
    dot_general x1, matrix products, on_device(): lax.dot_general(weight_part, stacked, (((0,), (0,)), ((), ())), preferred...  6.67 us
  transfers between devices with their start and end apart: 5, of which 2 were waited for; matrix products, arithmetic and copies ran while one was open for 15% of the time, Pallas kernels for 0%

commit v1 on v0

--- a/solution.py
+++ b/solution.py
@@ -50,7 +50,7 @@
         stacked, active, (((1,), (1,)), ((), ())), preferred_element_type=jnp.float32
     )
     positions = frames * lax.axis_size("tm") * rows * lax.axis_size("height") * cols
-    summed = lax.psum(local_sums, ("tm", "height"))
+    summed = lax.psum(lax.psum(local_sums, "height"), "tm")
     weight_grad = (summed / math.sqrt(positions)).reshape(chans, 27, total)
     sig = jax.nn.sigmoid(normed)
     slope = sig * (1.0 + normed * (1.0 - sig))

time: 247 us -> 282 us (1.14)
  waiting for transfers between devices: 67 us -> 104 us
    unnamed x3 -> x4, waiting for transfers between devices: 0.03 us -> 25.3 us
    psum x1 -> x2, waiting for transfers between devices: 66.4 us -> 78.6 us  [on_device(): summed = lax.psum(lax.psum(local_sums, 'height'), 'tm')]
    unnamed x36 -> x34, local copies, waits for them, and re-layouts: 30.9 us -> 30.9 us
  transfers between devices with their start and end apart: 5 -> 6, of which waited for: 2 -> 4; matrix products, arithmetic and copies ran while one was open for 15% -> 10% of each run, Pallas kernels for 0% -> 0%
where the time goes in v1:
time: 282 us; the launch traced here: 280 us
  waiting for transfers between devices  104 us (37%)
  local copies, waits for them, and re-layouts  82 us (29%)
  blocking collectives  41.4 us (15%)
  other arithmetic  17.6 us (6%)
  between operations  15.7 us (6%)
  matrix products  15.1 us (5%)
  starting transfers between devices  4.19 us (1%)
    psum x2, waiting for transfers between devices, on_device(): summed = lax.psum(lax.psum(local_sums, 'height'), 'tm')  78.6 us
    all_gather x1, blocking collectives, on_device(): whole_x = lax.all_gather(features, 'chan', axis=0, tiled=True)  31.4 us
    unnamed x34, local copies, waits for them, and re-layouts  30.9 us
    unnamed x4, waiting for transfers between devices  25.3 us
    another operation x2, local copies, waits for them, and re-layouts, on_device(): stacked = jnp.stack(taps, axis=1).reshape(chans * 27, -1)  21.9 us
    reshape x1, local copies, waits for them, and re-layouts, on_device(): stacked = jnp.stack(taps, axis=1).reshape(chans * 27, -1)  20.4 us
    psum x1, blocking collectives, on_device(): dots = lax.psum(jnp.sum(upstream * own_x, axis=0, keepdims=True), 'chan')  9.94 us
    dot_general x1, matrix products, on_device(): lax.dot_general(stacked, active, (((1,), (1,)), ((), ())), preferred_elem...  8.42 us
  transfers between devices with their start and end apart: 6, of which 4 were waited for; matrix products, arithmetic and copies ran while one was open for 10% of the time, Pallas kernels for 0%

profile of v1, /device:TPU:0, one launch (start us, length us, event | category | flops | bytes accessed | tf_op | source)
XLA Modules:
  0.0 280.4 jit_solution(10245791537675759909)
XLA Ops:
  8.0 1.3 collective-permute-start
  9.3 1.3 copy.16
  10.7 31.4 %all_gather.3 = bf16[384,2,4,160]{3,2,1,0:T(4,128)(2,1)S(1)} all-gather(bf16[96,2,4,160]{3,2,1,0:T(4,128)(2,1)S(1)} %copy.16), channel_id=1, replica_groups=mesh['tm'=4,'height'=2,'chan'=4] {'chan'}, dimensions={0}, use_global_device_ids=true | all-gather | bytes 1228800 | tf_op jit(solution)/shard_map/all_gather | solution.py:29
  42.1 1.4 copy.17
  43.9 1.0 constant_dynamic-update-slice_fusion.1
  45.0 1.3 collective-permute-start.1
  46.3 1.3 collective-permute-start.2
  47.6 1.4 multiply_convert_fusion
  50.0 0.8 fusion.53
  50.8 0.8 fusion.30
  52.4 0.8 fusion.51
  53.9 0.8 fusion.50
  54.7 0.8 fusion.49
  55.5 0.8 fusion.24
  56.3 0.8 fusion.48
  57.1 0.8 fusion.47
  57.9 0.8 fusion.27
  59.5 0.8 fusion.45
  60.3 0.8 fusion.44
  61.0 0.8 fusion.43
  61.8 0.8 fusion.42
  62.6 0.8 fusion.21
  63.4 0.8 fusion.41
  64.2 0.8 fusion.40
  65.0 0.8 fusion.39
  65.8 0.8 fusion.37
  66.5 0.8 fusion.36
  68.1 0.8 fusion.35
  68.8 0.8 fusion.34
  69.7 0.8 fusion.33
  71.2 21.2 %copy.18 = bf16[96,27,2,4,160]{4,3,2,1,0:T(4,128)(2,1)} copy(bf16[96,27,2,4,160]{0,4,3,2,1:T(8,128)(2,1)} %fusion.31) | data formatting | bytes 13271040 | tf_op jit(solution)/shard_map/stack | solution.py:48
  92.4 20.4 %reshape.67 = bf16[2592,1280]{1,0:T(8,128)(2,1)} reshape(bf16[96,27,2,4,160]{4,3,2,1,0:T(4,128)(2,1)} %copy.18) | data formatting | bytes 13271040 | tf_op jit(solution)/shard_map/reshape | solution.py:48
  112.8 8.4 %fusion.56 = f32[2592,384]{1,0:T(8,128)} fusion(bf16[2592,1280]{1,0:T(8,128)(2,1)} %reshape.67, bf16[384,1280]{0,1:T(8,128)(2,1)S(1)} %bitcast.128), kind=kOutput, calls=%fused_computation.102 | convolution fusion | flops 2548039680 | bytes 11599872 | tf_op jit(solution)/shard_map/dot_general | solution.py:49
  121.5 2.3 copy.19
  123.8 2.2 reshape.68
  126.0 6.6 %convolution_bitcast_fusion = f32[384,1280]{0,1:T(8,128)S(1)} fusion(bf16[2592,1280]{1,0:T(8,128)(2,1)} %reshape.67, bf16[2592,384]{1,0:T(8,128)(2,1)} %reshape.68), kind=kOutput, calls=%fused_computation.2 | convolution fusion | flops 2548039680 | bytes 10592256 | tf_op jit(solution)/shard_map/dot_general | solution.py:60
  132.7 1.9 copy.21
  134.6 17.5 %all-reduce.4.cloned.1.call-done = f32[2592,384]{1,0:T(8,128)} async-done(((f32[2592,384]{1,0:T(8,128)}), f32[2592,384]{1,0:T(8,128)}) %all-reduce.4.cloned.1.call-update) | async-done | bytes 3981328 | tf_op jit(solution)/shard_map/psum | solution.py:53
  152.3 1.7 negate_exponential_fusion
  154.0 25.2 %reduce-scatter.4.cloned.1.call-done = f32[96,1280]{1,0:T(8,128)} async-done(((f32[384,1280]{1,0:T(8,128)}), f32[96,1280]{1,0:T(8,128)}) %reduce-scatter.4.cloned.1.call-update) | async-done | bytes 491536
  179.2 2.2 copy.22
  181.4 2.3 fusion.13
  183.6 9.9 %psum.21 = f32[1280]{0:T(1024)S(1)} all-reduce(f32[1280]{0:T(1024)S(1)} %get-tuple-element.10), channel_id=1, replica_groups=mesh['tm'=4,'height'=2,'chan'=4] {'chan'}, use_global_device_ids=true, to_apply=%region_3.4 | all-reduce | flops 1280 | bytes 10240 | tf_op jit(solution)/shard_map/psum | solution.py:71
  193.6 2.3 fusion.12
  195.9 61.1 %all-reduce.6.cloned.1.call-done = f32[2592,384]{1,0:T(8,128)} async-done(((f32[2592,384]{1,0:T(8,128)}), f32[2592,384]{1,0:T(8,128)}) %all-reduce.6.cloned.1.call-update) | async-done | bytes 3981328 | tf_op jit(solution)/shard_map/psum | solution.py:53
  257.0 4.4 %broadcast_multiply_fusion = f32[2592,384]{1,0:T(8,128)} fusion(f32[2592,384]{1,0:T(8,128)} %all-reduce.6.cloned.1.call-done), kind=kLoop, calls=%fused_computation.4 | loop fusion | flops 995328 | bytes 7962624 | tf_op jit(solution)/shard_map/div | solution.py:54
  261.4 4.9 %reshape.70 = f32[96,27,384]{2,1,0:T(8,128)} reshape(f32[2592,384]{1,0:T(8,128)} %broadcast_multiply_fusion) | data formatting | bytes 7962624 | tf_op jit(solution)/shard_map/reshape | solution.py:54
  266.4 6.6 %copy.20 = f32[96,27,384]{2,0,1:T(8,128)} copy(f32[96,27,384]{2,1,0:T(8,128)} %reshape.70) | data formatting | bytes 7962624
  (30 shorter events, 5.6 us)
Async XLA Ops:
  8.0 144.1 %all-reduce.4.cloned.1.call-start = ((), (), s32[]{:S(2)}) async-start(), calls=%async_computation.1 | async-start | bytes 7962624 | tf_op jit(solution)/shard_map/psum | solution.py:53
  8.0 36.9 %collective-permute-start = (bf16[96,2,4,160]{0,3,2,1:T(8,128)(2,1)}, bf16[96,2,4,160]{0,3,2,1:T(8,128)(2,1)S(1)}, u32[]{:S(2)}, u32[]{:S(2)}) collective-permute-start(bf16[96,2,4,160]{0,3,2,1:T(8,128)(2,1)} %param.6), channel_id=1, source_target_pairs={{8,0},{16,8},{24,16},{9,1},{17,9},{25,17},{10,2},{18,10},{26,18},{... | collective-permute-start | bytes 737288 | tf_op jit(solution)/shard_map/ppermute | solution.py:11
  45.0 4.0 %collective-permute-start.1 = (bf16[96,4,1,160]{0,3,2,1:T(8,128)(2,1)S(1)}, bf16[96,4,1,160]{0,3,2,1:T(8,128)(2,1)S(1)}, u32[]{:S(2)}, u32[]{:S(2)}) collective-permute-start(bf16[96,4,1,160]{0,3,2,1:T(8,128)(2,1)S(1)} %get-tuple-element.14), channel_id=1, source_target_pairs={{0,4},{1,5},{2,6},{3,7},{8,12},{9,13},{10,14},{11,15},{16,20},{17,... | collective-permute-start | bytes 368648 | tf_op jit(solution)/shard_map/ppermute | solution.py:21
  46.3 3.3 %collective-permute-start.2 = (bf16[96,4,1,160]{0,3,2,1:T(8,128)(2,1)S(1)}, bf16[96,4,1,160]{0,3,2,1:T(8,128)(2,1)S(1)}, u32[]{:S(2)}, u32[]{:S(2)}) collective-permute-start(bf16[96,4,1,160]{0,3,2,1:T(8,128)(2,1)S(1)} %get-tuple-element.15), channel_id=1, source_target_pairs={{4,0},{5,1},{6,2},{7,3},{12,8},{13,9},{14,10},{15,11},{20,16},{21,... | collective-permute-start | bytes 368648 | tf_op jit(solution)/shard_map/ppermute | solution.py:22
  50.0 17.4 %copy-start = (bf16[96,2,4,160]{0,3,2,1:T(8,128)(2,1)S(1)}, bf16[96,2,4,160]{0,3,2,1:T(8,128)(2,1)}, u32[]{:S(2)}) copy-start(bf16[96,2,4,160]{0,3,2,1:T(8,128)(2,1)} %param.6) | copy-start | bytes 737284
  121.3 58.0 %reduce-scatter.4.cloned.1.call-start = ((), (), s32[]{:S(2)}) async-start(), calls=%async_computation.3 | async-start | bytes 2457600
  132.6 19.6 %copy-start.2 = (f32[384]{0:T(512)S(1)}, f32[384]{0:T(512)}, u32[]{:S(2)}) copy-start(f32[384]{0:T(512)} %param.8) | copy-start | bytes 4612
  132.6 19.6 %copy-start.3 = (f32[384]{0:T(512)S(1)}, f32[384]{0:T(512)}, u32[]{:S(2)}) copy-start(f32[384]{0:T(512)} %param.9) | copy-start | bytes 4612
  132.7 60.9 %copy-start.1 = (bf16[96,2,4,160]{0,3,2,1:T(8,128)(2,1)S(1)}, bf16[96,2,4,160]{0,3,2,1:T(8,128)(2,1)}, u32[]{:S(2)}) copy-start(bf16[96,2,4,160]{0,3,2,1:T(8,128)(2,1)} %param.6) | copy-start | bytes 737284
  134.6 122.5 %all-reduce.6.cloned.1.call-start = ((), (), s32[]{:S(2)}) async-start(), calls=%async_computation.2 | async-start | bytes 7962624 | tf_op jit(solution)/shard_map/psum | solution.py:53
Sparse Core Ops, SparseCore 0:
  121.4 30.6 all-reduce.3
  155.5 101.5 all-reduce.5
Sparse Core Ops, SparseCore 1:
  134.6 44.5 reduce-scatter.3
